TPU v7x, 256 devices: a whole 4x4x8 slice. The times are simulated.
256 devices in a mesh: row: 8 (over x, core), col: 32 (over z, y).
Axes of the slice: x: 4, y: 4, z: 8, core: 2. Of those that a mesh axis runs over, the one named last changes fastest.
Arguments:
- leaf_rhs: bfloat16 [6144, 128, 512], P(('row', 'col')), may hold values from -6 to 6
- leaf_inverse: bfloat16 [6144, 128, 128], P(('row', 'col')), as said below
- leaf_link: bfloat16 [6144, 128, 128], P(('row', 'col')), may hold values from -0.109375 to 0.109375
- leaf_parent: int32 [6144], P(('row', 'col')), may hold values from 0 to 255, as said below
- node_rhs: bfloat16 [256, 128, 512], P(('row', 'col')), may hold values from -6 to 6
- node_inverse: bfloat16 [256, 128, 128], P(('row', 'col')), as said below
- node_link: bfloat16 [256, 128, 128], P(('row', 'col')), may hold values from -0.25 to 0.25
- node_parent: int32 [256], P('row'), may hold values from 0 to 63, as said below
- middle_rhs: bfloat16 [64, 128, 512], P('row'), may hold values from -6 to 6
- middle_inverse: bfloat16 [64, 128, 128], P('row'), as said below
- middle_link: bfloat16 [64, 128, 128], P('row'), may hold values from -0.125 to 0.125
- middle_parent: int32 [64], P('row'), may hold values from 0 to 3
- top_rhs: bfloat16 [4, 128, 512], replicated, may hold values from -6 to 6
- top_inverse: bfloat16 [4, 128, 128], replicated, as said below
Outputs:
- leaf_result: bfloat16 [6144, 128, 512], P(('row', 'col'))
- node_result: bfloat16 [256, 128, 512], P(('row', 'col'))
- middle_result: bfloat16 [64, 128, 512], P('row')
- top_result: bfloat16 [4, 128, 512], replicated
Inputs may be any that keep to these rules, and one draw needn't show every extreme that they name: `leaf_parent`: the parent of a leaf held by the device at grid row r lies in block row r: it is r * 32 + c for some c below 32. `node_parent`: the parent of second-level supernode r * 32 + c is r * 8 + j for some j below 8. `leaf_inverse`: each block is lower triangular. `node_inverse`: each block is lower triangular. `middle_inverse`: each block is lower triangular. `top_inverse`: each block is lower triangular.
All inputs are finite; a program needn't handle non-finite values.
Results may differ from a plain program's by a relative error of at most 0.017.
Values may be sent and summed in bfloat16 or wider, within the bound.
No kernel may reach another device: no remote copies, remote signals or barrier semaphores. Data moves between devices by JAX's collectives and lax.ppermute only.
A program may use at most 128 MiB of HBM per device.

v0:
```python
import jax
import jax.numpy as jnp
from jax import lax
from jax.sharding import PartitionSpec as P


def apply_block(matrix, vectors):
    return jnp.einsum("nij,njr->nir", matrix, vectors, preferred_element_type=jnp.float32)


def apply_transposed(matrix, vectors):
    return jnp.einsum("nij,nir->njr", matrix, vectors, preferred_element_type=jnp.float32)


def slot_sums(targets, count, values):
    slots = lax.iota(jnp.int32, count)
    select = (slots[:, None] == targets[None, :]).astype(jnp.float32)
    return jnp.einsum("sk,kwr->swr", select, values, precision=lax.Precision.HIGHEST)


def local(
    leaf_rhs,
    leaf_inverse,
    leaf_link,
    leaf_parent,
    node_rhs,
    node_inverse,
    node_link,
    node_parent,
    middle_rhs,
    middle_inverse,
    middle_link,
    middle_parent,
    top_rhs,
    top_inverse,
):
    peers = lax.axis_size("col")
    col_index = lax.axis_index("col")
    width = leaf_rhs.shape[1]
    columns = leaf_rhs.shape[2]
    chunk = columns // peers
    middle_count = middle_rhs.shape[0]
    top_count = top_rhs.shape[0]
    leaf_target = leaf_parent % peers
    middle_target = node_parent % middle_count
    leaf_solved = apply_block(leaf_inverse, leaf_rhs).astype(jnp.bfloat16)
    leaf_update = apply_block(leaf_link, leaf_solved)
    outgoing = slot_sums(leaf_target, peers, leaf_update).astype(jnp.bfloat16)
    incoming = lax.all_to_all(outgoing, "col", 0, 0, tiled=True)
    node_sum = jnp.sum(incoming.astype(jnp.float32), axis=0, keepdims=True)
    node_y = (node_rhs.astype(jnp.float32) - node_sum).astype(jnp.bfloat16)
    node_solved = apply_block(node_inverse, node_y).astype(jnp.bfloat16)
    node_update = apply_block(node_link, node_solved)[0]
    pieces = node_update.reshape(width, peers, chunk).transpose(1, 0, 2)
    row_updates = lax.all_to_all(pieces, "col", 0, 0, tiled=True)
    middle_sum = slot_sums(middle_target, middle_count, row_updates)
    start = col_index * chunk
    middle_piece = lax.dynamic_slice_in_dim(middle_rhs, start, chunk, 2)
    middle_y = (middle_piece.astype(jnp.float32) - middle_sum).astype(jnp.bfloat16)
    middle_solved = apply_block(middle_inverse, middle_y).astype(jnp.bfloat16)
    top_term = slot_sums(middle_parent, top_count, apply_block(middle_link, middle_solved))
    top_sum = lax.psum(top_term, "row")
    top_piece = lax.dynamic_slice_in_dim(top_rhs, start, chunk, 2)
    top_y = (top_piece.astype(jnp.float32) - top_sum).astype(jnp.bfloat16)
    top_solved = apply_block(top_inverse, top_y).astype(jnp.bfloat16)
    top_part = apply_transposed(top_inverse, top_solved).astype(jnp.bfloat16)
    middle_w = (
        middle_solved.astype(jnp.float32) - apply_transposed(middle_link, top_part[middle_parent])
    ).astype(jnp.bfloat16)
    middle_part = apply_transposed(middle_inverse, middle_w).astype(jnp.bfloat16)
    parts = jnp.concatenate([middle_part, top_part], axis=0)
    gathered = lax.all_gather(parts, "col", axis=0, tiled=False)
    whole = gathered.transpose(1, 2, 0, 3).reshape(middle_count + top_count, width, columns)
    middle_result = whole[:middle_count]
    top_result = whole[middle_count:]
    own_target = lax.dynamic_slice_in_dim(middle_target, col_index, 1)
    node_w = (
        node_solved.astype(jnp.float32) - apply_transposed(node_link, middle_result[own_target])
    ).astype(jnp.bfloat16)
    node_result = apply_transposed(node_inverse, node_w).astype(jnp.bfloat16)
    row_result = lax.all_gather(node_result, "col", axis=0, tiled=True)
    leaf_w = (
        leaf_solved.astype(jnp.float32) - apply_transposed(leaf_link, row_result[leaf_target])
    ).astype(jnp.bfloat16)
    leaf_result = apply_transposed(leaf_inverse, leaf_w).astype(jnp.bfloat16)
    return (leaf_result, node_result, middle_result, top_result)


def solution(mesh):
    placed = (
        P(("row", "col"), None, None),
        P(("row", "col"), None, None),
        P(("row", "col"), None, None),
        P(("row", "col")),
        P(("row", "col"), None, None),
        P(("row", "col"), None, None),
        P(("row", "col"), None, None),
        P("row"),
        P("row", None, None),
        P("row", None, None),
        P("row", None, None),
        P("row"),
        P(),
        P(),
    )
    return jax.shard_map(
        local,
        mesh=mesh,
        in_specs=placed,
        out_specs=(
            P(("row", "col"), None, None),
            P(("row", "col"), None, None),
            P("row", None, None),
            P(),
        ),
        check_vma=False,
    )
```

profile of v0, /device:TPU:16, one launch (start us, length us, event | category | flops | bytes accessed | tf_op | source)
XLA Modules:
  0.0 383.2 jit_solution(12176339282254675530)
XLA Ops:
  7.2 1.9 copy-done
  9.1 2.1 convolution_convert_fusion.1
  11.2 1.7 copy-done.1
  12.8 3.7 convolution_bitcast_fusion
  16.5 6.7 %copy.50 = f32[24,128,512]{2,0,1:T(8,128)} copy(f32[24,128,512]{1,2,0:T(8,128)} %convolution_bitcast_fusion) | data formatting | bytes 12582912 | tf_op jit(solution)/shard_map/nij,njr->nir/dot_general | solution.py:8
  23.8 6.0 %convolution_convert_fusion = bf16[32,128,512]{2,0,1:T(8,128)(2,1)S(1)} fusion(f32[24,128,512]{2,0,1:T(8,128)} %copy.50, s32[24]{0:T(128)S(1)} %get-tuple-element.32), kind=kOutput, calls=%fused_computation.8 | convolution fusion | flops 606077696 | bytes 10485856 | tf_op jit(solution)/shard_map/sk,kwr->swr/dot_general | solution.py:18
  29.8 4.4 %copy.51 = bf16[32,128,512]{2,1,0:T(8,128)(2,1)} copy(bf16[32,128,512]{2,0,1:T(8,128)(2,1)S(1)} %convolution_convert_fusion) | data formatting | bytes 8388608 | tf_op jit(solution)/shard_map/convert_element_type | solution.py:48
  34.1 11.6 %all-to-all-start = ((bf16[32,128,512]{2,1,0:T(8,128)(2,1)}), bf16[32,128,512]{2,1,0:T(8,128)(2,1)}, u32[]{:S(2)}, u32[]{:S(2)}) async-start(bf16[32,128,512]{2,1,0:T(8,128)(2,1)} %copy.51), calls=%async_computation | async-start | bytes 8388608 | tf_op jit(solution)/shard_map/all_to_all | solution.py:49
  48.8 89.8 %all-to-all-done = bf16[32,128,512]{2,1,0:T(8,128)(2,1)} async-done(((bf16[32,128,512]{2,1,0:T(8,128)(2,1)}), bf16[32,128,512]{2,1,0:T(8,128)(2,1)}, u32[]{:S(2)}, u32[]{:S(2)}) %all-to-all-start) | async-done | bytes 4194336 | tf_op jit(solution)/shard_map/all_to_all | solution.py:49
  138.6 2.8 convert_reduce_fusion
  141.4 1.1 convolution_convert_fusion.3
  143.5 8.4 %all-to-all-start.1 = ((f32[32,128,16]{1,2,0:T(8,128)}), f32[32,128,16]{1,2,0:T(8,128)}, u32[]{:S(2)}, u32[]{:S(2)}) async-start(f32[32,128,16]{1,2,0:T(8,128)} %convolution_bitcast_fusion.1), calls=%async_computation.1 | async-start | bytes 524288 | tf_op jit(solution)/shard_map/all_to_all | solution.py:55
  153.9 9.5 %all-to-all-done.1 = f32[32,128,16]{1,2,0:T(8,128)} async-done(((f32[32,128,16]{1,2,0:T(8,128)}), f32[32,128,16]{1,2,0:T(8,128)}, u32[]{:S(2)}, u32[]{:S(2)}) %all-to-all-start.1) | async-done | bytes 262176 | tf_op jit(solution)/shard_map/all_to_all | solution.py:55
  163.3 1.2 fusion.8
  164.6 1.2 convolution_convert_fusion.5
  165.7 1.2 convolution_bitcast_fusion.2
  167.8 24.5 %psum.7 = f32[4,128,16]{1,0,2:T(4,128)S(1)} all-reduce(f32[4,128,16]{1,0,2:T(4,128)S(1)} %fusion.21), channel_id=1, replica_groups=mesh['row'=8,'col'=32] {'row'}, use_global_device_ids=true, to_apply=%region_1.2 | all-reduce | flops 8192 | bytes 65536 | tf_op jit(solution)/shard_map/psum | solution.py:62
  193.4 1.3 fusion.10
  195.7 1.2 dynamic_slice.11
  198.8 67.3 %all-gather.5.cloned.1.call-done = bf16[384,128,16]{1,2,0:T(8,128)(2,1)} async-done(((bf16[12,128,16]{1,2,0:T(8,128)(2,1)}), bf16[384,128,16]{1,2,0:T(8,128)(2,1)}) %all-gather.5.cloned.1.call-update) | async-done | bytes 1572880 | tf_op jit(solution)/shard_map/all_gather | solution.py:72
  266.1 1.4 slice.29
  267.5 1.2 copy.58
  268.7 1.9 convolution_convert_fusion.2
  270.6 2.3 copy.66
  272.9 1.9 slice.30
  275.6 1.9 copy.63
  277.4 2.0 copy.67
  279.5 74.3 %all-gather.7.cloned.1.call-done = bf16[4096,512]{0,1:T(8,128)(2,1)} async-done(((bf16[128,512]{0,1:T(8,128)(2,1)}), bf16[4096,512]{0,1:T(8,128)(2,1)}) %all-gather.7.cloned.1.call-update) | async-done | bytes 4194320 | tf_op jit(solution)/shard_map/all_gather | solution.py:81
  353.8 6.5 %copy.72 = bf16[4096,512]{1,0:T(8,128)(2,1)} copy(bf16[4096,512]{0,1:T(8,128)(2,1)} %all-gather.7.cloned.1.call-done) | data formatting | bytes 8388608 | tf_op jit(solution)/shard_map/all_gather | solution.py:81
  360.3 4.7 %gather_fusion.1 = bf16[24,128,512]{2,1,0:T(8,128)(2,1)} fusion(bf16[32,128,512]{2,1,0:T(8,128)(2,1)} %bitcast.82, s32[1024]{0:T(1024)S(1)} %pad_clamp_fusion), kind=kCustom, calls=%fused_computation.1 | custom fusion | bytes 6291552 | tf_op jit(solution)/shard_map/gather | solution.py:83
  365.0 6.8 %convert_bitcast_fusion = bf16[24,128,512]{1,2,0:T(8,128)(2,1)} fusion(bf16[24,128,128]{2,1,0:T(8,128)(2,1)} %param.15, bf16[24,128,512]{2,1,0:T(8,128)(2,1)} %copy-done.1, bf16[24,128,512]{2,1,0:T(8,128)(2,1)} %gather_fusion.1, bf16[24,128,128]{2,1,0:T(8,128)(2,1)} %param.16), kind=kOutput, calls=%fused_computation.6 | convolution fusion | flops 811597824 | bytes 11010048 | tf_op jit(solution)/shard_map/nij,nir->njr/dot_general | solution.py:12
  371.7 4.6 %copy.64 = bf16[24,128,512]{2,1,0:T(8,128)(2,1)} copy(bf16[24,128,512]{1,2,0:T(8,128)(2,1)} %convert_bitcast_fusion) | data formatting | bytes 6291456
  (42 shorter events, 10.0 us)
Async XLA Ops:
  7.2 1.9 copy-start
  7.2 5.6 %copy-start.2 = (bf16[24,128,128]{2,1,0:T(8,128)(2,1)S(1)}, bf16[24,128,128]{2,1,0:T(8,128)(2,1)}, u32[]{:S(2)}) copy-start(bf16[24,128,128]{2,1,0:T(8,128)(2,1)} %param.16) | copy-start | bytes 2359300
  11.2 1.7 copy-start.1
  16.5 6.7 %copy-start.11 = (s32[24]{0:T(128)S(1)}, s32[24]{0:T(128)}, u32[]{:S(2)}) copy-start(s32[24]{0:T(128)} %param.17) | copy-start | bytes 292
  34.1 104.5 %all-to-all-start = ((bf16[32,128,512]{2,1,0:T(8,128)(2,1)}), bf16[32,128,512]{2,1,0:T(8,128)(2,1)}, u32[]{:S(2)}, u32[]{:S(2)}) async-start(bf16[32,128,512]{2,1,0:T(8,128)(2,1)} %copy.51), calls=%async_computation | async-start | bytes 8388608 | tf_op jit(solution)/shard_map/all_to_all | solution.py:49
  45.8 95.6 %copy-start.5 = (bf16[1,128,128]{2,1,0:T(8,128)(2,1)S(1)}, bf16[1,128,128]{2,1,0:T(8,128)(2,1)}, u32[]{:S(2)}) copy-start(bf16[1,128,128]{2,1,0:T(8,128)(2,1)} %param.19) | copy-start | bytes 98308
  45.8 96.8 %copy-start.6 = (bf16[1,128,128]{2,1,0:T(8,128)(2,1)S(1)}, bf16[1,128,128]{2,1,0:T(8,128)(2,1)}, u32[]{:S(2)}) copy-start(bf16[1,128,128]{2,1,0:T(8,128)(2,1)} %param.20) | copy-start | bytes 98308
  48.8 143.5 %copy-start.8 = (bf16[4,128,16]{1,0,2:T(4,128)(2,1)S(1)}, bf16[4,128,16]{1,0,2:T(4,128)(2,1)}, u32[]{:S(2)}) copy-start(bf16[4,128,16]{1,0,2:T(4,128)(2,1)} %copy.74) | copy-start | bytes 49156
  48.8 143.5 %copy-start.4 = (bf16[4,128,128]{2,1,0:T(8,128)(2,1)S(1)}, bf16[4,128,128]{2,1,0:T(8,128)(2,1)}, u32[]{:S(2)}) copy-start(bf16[4,128,128]{2,1,0:T(8,128)(2,1)} %param.27) | copy-start | bytes 393220
  143.5 19.9 %all-to-all-start.1 = ((f32[32,128,16]{1,2,0:T(8,128)}), f32[32,128,16]{1,2,0:T(8,128)}, u32[]{:S(2)}, u32[]{:S(2)}) async-start(f32[32,128,16]{1,2,0:T(8,128)} %convolution_bitcast_fusion.1), calls=%async_computation.1 | async-start | bytes 524288 | tf_op jit(solution)/shard_map/all_to_all | solution.py:55
  151.9 114.2 %all-gather.5.cloned.1.call-start = ((), (), s32[]{:S(2)}) async-start(), calls=%async_computation.2 | async-start | bytes 1622016 | tf_op jit(solution)/shard_map/all_gather | solution.py:72
  153.9 11.9 %copy-start.9 = (s32[32]{0:T(128)}, s32[32]{0:T(128)S(1)}, u32[]{:S(2)}) copy-start(s32[32]{0:T(128)S(1)} %and_select_fusion) | copy-start | bytes 388
  192.3 76.4 %copy-start.7 = (bf16[1,128,128]{2,1,0:T(8,128)(2,1)S(1)}, bf16[1,128,128]{2,1,0:T(8,128)(2,1)}, u32[]{:S(2)}) copy-start(bf16[1,128,128]{2,1,0:T(8,128)(2,1)} %param.20) | copy-start | bytes 98308
  192.6 78.0 %copy-start.10 = (s32[24]{0:T(128)S(1)}, s32[24]{0:T(128)}, u32[]{:S(2)}) copy-start(s32[24]{0:T(128)} %get-tuple-element.31) | copy-start | bytes 292
  195.4 158.3 %all-gather.7.cloned.1.call-start = ((), (), s32[]{:S(2)}) async-start(), calls=%async_computation.3 | async-start | bytes 4325376 | tf_op jit(solution)/shard_map/all_gather | solution.py:81
  270.6 4.2 %copy-start.3 = (bf16[512,128]{1,0:T(8,128)(2,1)S(1)}, bf16[512,128]{1,0:T(8,128)(2,1)}, u32[]{:S(2)}) copy-start(bf16[512,128]{1,0:T(8,128)(2,1)} %convolution_convert_fusion.2) | copy-start | bytes 393220
Sparse Core Ops, SparseCore 0:
  195.5 70.5 all-gather.4
  270.7 82.9 all-gather.6
where the time goes:
time: 384 us; the launch traced here: 383 us
  waiting for transfers between devices  241 us (63%)
  local copies, waits for them, and re-layouts  46.9 us (12%)
  matrix products  28.5 us (7%)
  blocking collectives  24.5 us (6%)
  starting transfers between devices  20.3 us (5%)
  between operations  16.2 us (4%)
  other arithmetic  5.91 us (2%)
    all_to_all x1, waiting for transfers between devices, local(): incoming = lax.all_to_all(outgoing, 'col', 0, 0, tiled=True)  89.8 us
    all_gather x1, waiting for transfers between devices, local(): row_result = lax.all_gather(node_result, 'col', axis=0, tiled=True)  74.3 us
    all_gather x1, waiting for transfers between devices, local(): gathered = lax.all_gather(parts, 'col', axis=0, tiled=False)  67.3 us
    psum x1, blocking collectives, local(): top_sum = lax.psum(top_term, 'row')  24.5 us
    unnamed x30, local copies, waits for them, and re-layouts  14.1 us
    all_to_all x1, starting transfers between devices, local(): incoming = lax.all_to_all(outgoing, 'col', 0, 0, tiled=True)  11.6 us
    dot_general x4, matrix products, apply_transposed(): jnp.einsum('nij,nir->njr', matrix, vectors, preferred_element_type=jnp.fl...  10.2 us
    dot_general x6, matrix products, apply_block(): jnp.einsum('nij,njr->nir', matrix, vectors, preferred_element_type=jnp.fl...  10.2 us
  transfers between devices with their start and end apart: 4, of which 4 were waited for; matrix products, arithmetic and copies ran while one was open for 4% of the time, Pallas kernels for 0%

commit v1 on v0

--- a/solution.py
+++ b/solution.py
@@ -78,7 +78,9 @@
         node_solved.astype(jnp.float32) - apply_transposed(node_link, middle_result[own_target])
     ).astype(jnp.bfloat16)
     node_result = apply_transposed(node_inverse, node_w).astype(jnp.bfloat16)
-    row_result = lax.all_gather(node_result, "col", axis=0, tiled=True)
+    row_result = jnp.concatenate(
+        lax.all_to_all(jnp.stack([node_result] * lax.axis_size("col")), "col", 0, 0), axis=0
+    )
     leaf_w = (
         leaf_solved.astype(jnp.float32) - apply_transposed(leaf_link, row_result[leaf_target])
     ).astype(jnp.bfloat16)

time: 384 us -> 396 us (1.031)
  starting transfers between devices: 20.3 us -> 28 us
  waiting for transfers between devices: 241 us -> 248 us
  local copies, waits for them, and re-layouts: 46.9 us -> 42.9 us
    all_to_all x0 -> x1, waiting for transfers between devices: none -> 80.8 us  [local(): lax.all_to_all(jnp.stack([node_result] * lax.axis_size('col')), 'col', 0, 0)]
    all_gather x1 -> x0, waiting for transfers between devices: 74.3 us -> none  [local(): row_result = lax.all_gather(node_result, 'col', axis=0, tiled=True)]
    all_to_all x0 -> x1, starting transfers between devices: none -> 7.87 us  [local(): lax.all_to_all(jnp.stack([node_result] * lax.axis_size('col')), 'col', 0, 0)]
    all_gather x1 -> x0, local copies, waits for them, and re-layouts: 6.5 us -> none  [local(): row_result = lax.all_gather(node_result, 'col', axis=0, tiled=True)]
    unnamed x30 -> x28, local copies, waits for them, and re-layouts: 14.1 us -> 14.1 us
where the time goes in v1:
time: 396 us; the launch traced here: 393 us
  waiting for transfers between devices  248 us (63%)
  local copies, waits for them, and re-layouts  42.9 us (11%)
  starting transfers between devices  28 us (7%)
  matrix products  27.8 us (7%)
  blocking collectives  24.5 us (6%)
  between operations  16.2 us (4%)
  other arithmetic  5.93 us (1%)
    all_to_all x1, waiting for transfers between devices, local(): incoming = lax.all_to_all(outgoing, 'col', 0, 0, tiled=True)  89.8 us
    all_to_all x1, waiting for transfers between devices, local(): lax.all_to_all(jnp.stack([node_result] * lax.axis_size('col')), 'col', 0, 0)  80.8 us
    all_gather x1, waiting for transfers between devices, local(): gathered = lax.all_gather(parts, 'col', axis=0, tiled=False)  67.5 us
    psum x1, blocking collectives, local(): top_sum = lax.psum(top_term, 'row')  24.5 us
    unnamed x28, local copies, waits for them, and re-layouts  14.1 us
    all_to_all x1, starting transfers between devices, local(): incoming = lax.all_to_all(outgoing, 'col', 0, 0, tiled=True)  11.7 us
    dot_general x6, matrix products, apply_block(): jnp.einsum('nij,njr->nir', matrix, vectors, preferred_element_type=jnp.fl...  10.2 us
    dot_general x4, matrix products, apply_transposed(): jnp.einsum('nij,nir->njr', matrix, vectors, preferred_element_type=jnp.fl...  9.55 us
  transfers between devices with their start and end apart: 4, of which 4 were waited for; matrix products, arithmetic and copies ran while one was open for 4% of the time, Pallas kernels for 0%

profile of v1, /device:TPU:16, one launch (start us, length us, event | category | flops | bytes accessed | tf_op | source)
XLA Modules:
  0.0 392.8 jit_solution(4750883680844627280)
XLA Ops:
  7.2 1.9 copy-done
  9.1 2.1 convolution_convert_fusion.1
  11.2 1.7 copy-done.1
  12.8 3.7 convolution_bitcast_fusion
  16.5 6.7 %copy.69 = f32[24,128,512]{2,0,1:T(8,128)} copy(f32[24,128,512]{1,2,0:T(8,128)} %convolution_bitcast_fusion) | data formatting | bytes 12582912 | tf_op jit(solution)/shard_map/nij,njr->nir/dot_general | solution.py:8
  23.8 6.0 %convolution_convert_fusion = bf16[32,128,512]{2,0,1:T(8,128)(2,1)S(1)} fusion(f32[24,128,512]{2,0,1:T(8,128)} %copy.69, s32[24]{0:T(128)S(1)} %get-tuple-element.36), kind=kOutput, calls=%fused_computation.8 | convolution fusion | flops 606077696 | bytes 10485856 | tf_op jit(solution)/shard_map/sk,kwr->swr/dot_general | solution.py:18
  29.8 4.4 %copy.70 = bf16[32,128,512]{2,1,0:T(8,128)(2,1)} copy(bf16[32,128,512]{2,0,1:T(8,128)(2,1)S(1)} %convolution_convert_fusion) | data formatting | bytes 8388608 | tf_op jit(solution)/shard_map/convert_element_type | solution.py:48
  34.1 11.7 %all-to-all-start = ((bf16[32,128,512]{2,1,0:T(8,128)(2,1)}), bf16[32,128,512]{2,1,0:T(8,128)(2,1)}, u32[]{:S(2)}, u32[]{:S(2)}) async-start(bf16[32,128,512]{2,1,0:T(8,128)(2,1)} %copy.70), calls=%async_computation | async-start | bytes 8388608 | tf_op jit(solution)/shard_map/all_to_all | solution.py:49
  48.8 89.8 %all-to-all-done = bf16[32,128,512]{2,1,0:T(8,128)(2,1)} async-done(((bf16[32,128,512]{2,1,0:T(8,128)(2,1)}), bf16[32,128,512]{2,1,0:T(8,128)(2,1)}, u32[]{:S(2)}, u32[]{:S(2)}) %all-to-all-start) | async-done | bytes 4194336 | tf_op jit(solution)/shard_map/all_to_all | solution.py:49
  138.6 2.8 convert_reduce_fusion
  143.5 8.4 %all-to-all-start.1 = ((f32[32,128,16]{1,2,0:T(8,128)}), f32[32,128,16]{1,2,0:T(8,128)}, u32[]{:S(2)}, u32[]{:S(2)}) async-start(f32[32,128,16]{1,2,0:T(8,128)} %convolution_bitcast_fusion.1), calls=%async_computation.1 | async-start | bytes 524288 | tf_op jit(solution)/shard_map/all_to_all | solution.py:55
  153.9 9.5 %all-to-all-done.1 = f32[32,128,16]{1,2,0:T(8,128)} async-done(((f32[32,128,16]{1,2,0:T(8,128)}), f32[32,128,16]{1,2,0:T(8,128)}, u32[]{:S(2)}, u32[]{:S(2)}) %all-to-all-start.1) | async-done | bytes 262176 | tf_op jit(solution)/shard_map/all_to_all | solution.py:55
  163.3 1.2 fusion.8
  164.6 1.2 convolution_convert_fusion.5
  165.7 1.2 convolution_bitcast_fusion.2
  167.8 24.5 %psum.7 = f32[4,128,16]{1,0,2:T(4,128)S(1)} all-reduce(f32[4,128,16]{1,0,2:T(4,128)S(1)} %fusion.21), channel_id=1, replica_groups=mesh['row'=8,'col'=32] {'row'}, use_global_device_ids=true, to_apply=%region_1.2 | all-reduce | flops 8192 | bytes 65536 | tf_op jit(solution)/shard_map/psum | solution.py:62
  193.3 1.3 fusion.10
  195.3 1.3 dynamic_slice.11
  198.5 67.5 %all-gather.3.cloned.1.call-done = bf16[384,128,16]{1,2,0:T(8,128)(2,1)} async-done(((bf16[12,128,16]{1,2,0:T(8,128)(2,1)}), bf16[384,128,16]{1,2,0:T(8,128)(2,1)}) %all-gather.3.cloned.1.call-update) | async-done | bytes 1572880 | tf_op jit(solution)/shard_map/all_gather | solution.py:72
  266.0 1.4 slice.29
  267.4 1.2 copy.77
  268.6 1.2 convolution_convert_fusion.2
  269.9 2.4 stack.2
  272.3 7.9 %all-to-all-start.2 = ((bf16[32,1,128,512]{3,2,1,0:T(8,128)(2,1)}), bf16[32,1,128,512]{3,2,1,0:T(8,128)(2,1)}, u32[]{:S(2)}, u32[]{:S(2)}) async-start(bf16[32,1,128,512]{3,2,1,0:T(8,128)(2,1)} %stack.2), calls=%async_computation.2 | async-start | bytes 8388608 | tf_op jit(solution)/shard_map/all_to_all | solution.py:82
  280.2 2.3 copy.85
  282.5 1.9 slice.30
  285.2 1.9 copy.82
  287.1 2.0 copy.86
  289.1 80.8 %all-to-all-done.2 = bf16[32,1,128,512]{3,2,1,0:T(8,128)(2,1)} async-done(((bf16[32,1,128,512]{3,2,1,0:T(8,128)(2,1)}), bf16[32,1,128,512]{3,2,1,0:T(8,128)(2,1)}, u32[]{:S(2)}, u32[]{:S(2)}) %all-to-all-start.2) | async-done | bytes 4194336 | tf_op jit(solution)/shard_map/all_to_all | solution.py:82
  369.9 4.7 %gather_fusion.1 = bf16[24,128,512]{2,1,0:T(8,128)(2,1)} fusion(bf16[32,128,512]{2,1,0:T(8,128)(2,1)} %bitcast.20, s32[1024]{0:T(1024)S(1)} %pad_clamp_fusion), kind=kCustom, calls=%fused_computation.1 | custom fusion | bytes 6291552 | tf_op jit(solution)/shard_map/gather | solution.py:85
  374.6 6.7 %convert_bitcast_fusion = bf16[24,128,512]{1,2,0:T(8,128)(2,1)} fusion(bf16[24,128,128]{2,1,0:T(8,128)(2,1)} %param.15, bf16[24,128,512]{2,1,0:T(8,128)(2,1)} %copy-done.1, bf16[24,128,512]{2,1,0:T(8,128)(2,1)} %gather_fusion.1, bf16[24,128,128]{2,1,0:T(8,128)(2,1)} %param.16), kind=kOutput, calls=%fused_computation.6 | convolution fusion | flops 811597824 | bytes 11010048 | tf_op jit(solution)/shard_map/nij,nir->njr/dot_general | solution.py:12
  381.3 4.6 %copy.83 = bf16[24,128,512]{2,1,0:T(8,128)(2,1)} copy(bf16[24,128,512]{1,2,0:T(8,128)(2,1)} %convert_bitcast_fusion) | data formatting | bytes 6291456
  (40 shorter events, 10.9 us)
Async XLA Ops:
  7.2 1.9 copy-start
  7.2 5.6 %copy-start.2 = (bf16[24,128,128]{2,1,0:T(8,128)(2,1)S(1)}, bf16[24,128,128]{2,1,0:T(8,128)(2,1)}, u32[]{:S(2)}) copy-start(bf16[24,128,128]{2,1,0:T(8,128)(2,1)} %param.16) | copy-start | bytes 2359300
  11.2 1.7 copy-start.1
  16.5 6.7 %copy-start.10 = (s32[24]{0:T(128)S(1)}, s32[24]{0:T(128)}, u32[]{:S(2)}) copy-start(s32[24]{0:T(128)} %param.17) | copy-start | bytes 292
  34.1 104.5 %all-to-all-start = ((bf16[32,128,512]{2,1,0:T(8,128)(2,1)}), bf16[32,128,512]{2,1,0:T(8,128)(2,1)}, u32[]{:S(2)}, u32[]{:S(2)}) async-start(bf16[32,128,512]{2,1,0:T(8,128)(2,1)} %copy.70), calls=%async_computation | async-start | bytes 8388608 | tf_op jit(solution)/shard_map/all_to_all | solution.py:49
  45.8 95.6 %copy-start.4 = (bf16[1,128,128]{2,1,0:T(8,128)(2,1)S(1)}, bf16[1,128,128]{2,1,0:T(8,128)(2,1)}, u32[]{:S(2)}) copy-start(bf16[1,128,128]{2,1,0:T(8,128)(2,1)} %param.19) | copy-start | bytes 98308
  45.8 96.7 %copy-start.5 = (bf16[1,128,128]{2,1,0:T(8,128)(2,1)S(1)}, bf16[1,128,128]{2,1,0:T(8,128)(2,1)}, u32[]{:S(2)}) copy-start(bf16[1,128,128]{2,1,0:T(8,128)(2,1)} %param.20) | copy-start | bytes 98308
  48.8 143.5 %copy-start.7 = (bf16[4,128,16]{1,0,2:T(4,128)(2,1)S(1)}, bf16[4,128,16]{1,0,2:T(4,128)(2,1)}, u32[]{:S(2)}) copy-start(bf16[4,128,16]{1,0,2:T(4,128)(2,1)} %copy.92) | copy-start | bytes 49156
  48.8 143.5 %copy-start.3 = (bf16[4,128,128]{2,1,0:T(8,128)(2,1)S(1)}, bf16[4,128,128]{2,1,0:T(8,128)(2,1)}, u32[]{:S(2)}) copy-start(bf16[4,128,128]{2,1,0:T(8,128)(2,1)} %param.27) | copy-start | bytes 393220
  143.5 19.9 %all-to-all-start.1 = ((f32[32,128,16]{1,2,0:T(8,128)}), f32[32,128,16]{1,2,0:T(8,128)}, u32[]{:S(2)}, u32[]{:S(2)}) async-start(f32[32,128,16]{1,2,0:T(8,128)} %convolution_bitcast_fusion.1), calls=%async_computation.1 | async-start | bytes 524288 | tf_op jit(solution)/shard_map/all_to_all | solution.py:55
  151.9 114.1 %all-gather.3.cloned.1.call-start = ((), (), s32[]{:S(2)}) async-start(), calls=%async_computation.3 | async-start | bytes 1622016 | tf_op jit(solution)/shard_map/all_gather | solution.py:72
  153.9 11.9 %copy-start.8 = (s32[32]{0:T(128)}, s32[32]{0:T(128)S(1)}, u32[]{:S(2)}) copy-start(s32[32]{0:T(128)S(1)} %and_select_fusion) | copy-start | bytes 388
  192.3 76.3 %copy-start.6 = (bf16[1,128,128]{2,1,0:T(8,128)(2,1)S(1)}, bf16[1,128,128]{2,1,0:T(8,128)(2,1)}, u32[]{:S(2)}) copy-start(bf16[1,128,128]{2,1,0:T(8,128)(2,1)} %param.20) | copy-start | bytes 98308
  272.3 7.9 %copy-start.9 = (s32[24]{0:T(128)S(1)}, s32[24]{0:T(128)}, u32[]{:S(2)}) copy-start(s32[24]{0:T(128)} %get-tuple-element.35) | copy-start | bytes 292
  272.3 97.5 %all-to-all-start.2 = ((bf16[32,1,128,512]{3,2,1,0:T(8,128)(2,1)}), bf16[32,1,128,512]{3,2,1,0:T(8,128)(2,1)}, u32[]{:S(2)}, u32[]{:S(2)}) async-start(bf16[32,1,128,512]{3,2,1,0:T(8,128)(2,1)} %stack.2), calls=%async_computation.2 | async-start | bytes 8388608 | tf_op jit(solution)/shard_map/all_to_all | solution.py:82
Sparse Core Ops, SparseCore 0:
  195.4 70.5 all-gather.2
